TPU v7x, 32 devices: a whole 2x2x4 slice. The times are simulated.
32 devices in a mesh: patch: 8 (over z, y), band: 4 (over x, core).
Axes of the slice: x: 2, y: 2, z: 4, core: 2. Of those that a mesh axis runs over, the one named last changes fastest.
Arguments:
- exposures: float32 [64, 256, 128], P(('band', 'patch')), parts along dimension 0, may hold values from -6 to 6
- variance: float32 [64, 256, 128], P(('band', 'patch')), parts along dimension 0, may hold values from 0.01 to 60, as said below
- mask_bits: int32 [64, 256, 128], P(('band', 'patch')), parts along dimension 0, may hold values from 0 to 4095
- kernel_coeffs: float32 [64, 27, 6], P(('band', 'patch')), parts along dimension 0, may hold values from -3 to 3
- ccd_visit: int32 [64, 1], P(('band', 'patch')), parts along dimension 0, may hold values from 0 to 7
- strip_patch: int32 [2048, 1], P(('band', 'patch')), parts along dimension 0, may hold values from 0 to 7, as said below
- strip_row: int32 [2048], P(('band', 'patch')), parts along dimension 0, may hold values from 0 to 120
- strip_col: int32 [2048], P(('band', 'patch')), parts along dimension 0, may hold values from 0 to 384
Outputs:
- coadd_image: float32 [32, 128, 512], P(('band', 'patch')), parts along dimension 0
- weight_map: float32 [32, 128, 512], P(('band', 'patch')), parts along dimension 0
There are 4 independent parts, one for each index of `band`. A program takes and returns all parts, laid end to end along the dimension named above; each array names one. Nothing has to cross between parts.
Inputs may be any that keep to these rules, and one draw needn't show every extreme that they name: `variance`: Positive. `ccd_visit`: every visit has at least one CCD. `strip_patch`: among the strips of one device (aligned blocks of 64 rows) no patch is named more than 16 times; one patch is named exactly 16 times in every block.
All inputs are finite; a program needn't handle non-finite values.
Results may differ from a plain program's by a relative error of at most 0.00011.
Values sent between devices are 32-bit elements; how exact they have to be, the bound alone decides.
No kernel may reach another device: no remote copies, remote signals or barrier semaphores. Data moves between devices by JAX's collectives and lax.ppermute only.
A program may use at most 64 MiB of HBM per device.

v0:
```python
import math
import jax
import numpy as np
import jax.numpy as jnp
from jax import lax
from jax.sharding import PartitionSpec as P

PH = 128
PW = 512
KS = 21
VISITS = 8
gauss_widths = (0.75, 1.5, 3.0)
largest_value = lax.Precision.HIGHEST
mxu_value = lax.Precision.HIGH


def tap_table(kernel_half_width):
    support = np.arange(-kernel_half_width, kernel_half_width + 1).astype(np.float64)
    tables = []
    for spread in gauss_widths:
        s32 = float(np.float32(spread))
        gauss_total = np.sum(np.exp(-support * support / (2.0 * s32 * s32)))
        profile = np.exp(-support * support / (2.0 * s32 * s32)) / gauss_total
        scaled = support / s32
        tables.append(np.stack([profile, profile * scaled, profile * scaled * scaled]))
    return np.stack(tables)


def row_blocks(block_rows, window_rows, kernel_half_width):
    taps = tap_table(kernel_half_width).reshape(9, 2 * kernel_half_width + 1)
    out = np.zeros((9, block_rows, window_rows), np.float64)
    for i in range(block_rows):
        out[:, i, i : i + 2 * kernel_half_width + 1] = taps
    return out.astype(np.float32)


def column_ops(column_count, kernel_half_width):
    taps = tap_table(kernel_half_width)
    out = np.zeros((3, 3, column_count, column_count), np.float64)
    for y in range(column_count):
        lo = max(0, y - kernel_half_width)
        hi = min(column_count, y + kernel_half_width + 1)
        for x in range(lo, hi):
            out[:, :, y, x] = taps[:, :, y - x + kernel_half_width]
    return out.astype(np.float32)


def convolve_all(exposures, kernel_coeffs):
    kernel_half_width = KS // 2
    n, height, columns = exposures.shape
    block = 8
    blocks = height // block
    span = 2 * kernel_half_width + block
    reach = -(-span // block)
    total_rows = (blocks + reach - 1) * block
    padded = jnp.pad(
        exposures, ((0, 0), (kernel_half_width, total_rows - height - kernel_half_width), (0, 0))
    ).reshape(n, blocks + reach - 1, block, columns)
    windows = jnp.concatenate([padded[:, j : j + blocks] for j in range(reach)], axis=2)
    rows = jnp.asarray(row_blocks(block, reach * block, kernel_half_width))
    smooth = jnp.einsum("kit,nqtx->nqkix", rows, windows, precision=mxu_value)
    col_ops = jnp.asarray(column_ops(columns, kernel_half_width))
    x_line = 2.0 * jnp.arange(columns).astype(jnp.float32) / (columns - 1) - 1.0
    coef = kernel_coeffs.reshape(n, 3, 3, 3, 6)
    c = [coef[..., p, None] for p in range(6)]
    fx = jnp.stack(
        [
            c[0] + c[1] * x_line + c[3] * (x_line * x_line),
            c[2] + c[4] * x_line,
            jnp.broadcast_to(c[5], c[0].shape[:-1] + (columns,)),
        ],
        axis=4,
    )
    mixed = jnp.sum(col_ops[None, :, None, :, :, None, :] * fx[:, :, :, :, None, :, :], axis=3)
    mixed = mixed.reshape(n, 9, columns, 3 * columns)
    fields = jnp.einsum("nqkiy,nkyz->nqiz", smooth, mixed, precision=mxu_value)
    fields = fields.reshape(n, height, 3 * columns)
    y_line = (2.0 * jnp.arange(height).astype(jnp.float32) / (height - 1) - 1.0)[None, :, None]
    return (
        fields[:, :, :columns]
        + y_line * fields[:, :, columns : 2 * columns]
        + y_line * y_line * fields[:, :, 2 * columns :]
    )


def place_slots(flux_flat, weight_flat, offsets, patch_rows, patch_cols):
    slot_total, strip_rows, columns = flux_flat.shape
    group = math.gcd(slot_total, 16)
    pairs = jnp.stack([flux_flat, weight_flat], axis=1).reshape(
        slot_total // group, group, 2, strip_rows, columns
    )
    grouped_offsets = offsets.reshape(slot_total // group, group, offsets.shape[1])
    target_cols = jnp.arange(patch_cols)
    source_cols = jnp.arange(columns)
    target_rows = jnp.arange(patch_rows)
    source_rows = jnp.arange(strip_rows)

    def place_group(total, item):
        pixel_block_tile, block_offsets = item
        column_selection = (
            target_cols[None, None, :]
            == block_offsets[:, 1][:, None, None] + source_cols[None, :, None]
        ).astype(jnp.float32)
        row_select = (
            target_rows[None, :, None]
            == block_offsets[:, 0][:, None, None] + source_rows[None, None, :]
        ).astype(jnp.float32)
        broadened_width = jnp.einsum(
            "vmwn,vny->vmwy", pixel_block_tile, column_selection, precision=largest_value
        )
        return (
            total
            + jnp.einsum("gri,gkip->krp", row_select, broadened_width, precision=largest_value),
            None,
        )

    start = jnp.zeros((2, patch_rows, patch_cols), jnp.float32)
    placed, _ = lax.scan(place_group, start, (pairs, grouped_offsets))
    return (placed[0], placed[1])


def shards(
    exposures, variance, mask_bits, kernel_coeffs, ccd_visit, strip_patch, strip_row, strip_col
):
    ccd_count, height, columns = exposures.shape
    strip_total = strip_patch.shape[0]
    per_ccd = strip_total // ccd_count
    strip_rows = height // per_ccd
    devices = lax.axis_size("patch")
    capacity = 2 * strip_total // devices
    usable = (jnp.bitwise_and(mask_bits, 3) != 3).astype(jnp.float32)
    visit_hot = (ccd_visit == jnp.arange(VISITS)[None, :]).astype(jnp.float32)
    local_count = jnp.sum(jnp.sum(usable, axis=(1, 2))[:, None] * visit_hot, axis=0)
    local_load = jnp.sum(jnp.sum(usable * variance, axis=(1, 2))[:, None] * visit_hot, axis=0)
    destination = strip_patch[:, 0]
    strip_ids = jnp.arange(strip_total)
    earlier = strip_ids[None, :] < strip_ids[:, None]
    same_target = destination[None, :] == destination[:, None]
    slot_rank = jnp.sum(jnp.logical_and(earlier, same_target).astype(jnp.int32), axis=1)
    slot_index = destination * capacity + slot_rank
    slot_total = devices * capacity
    chooser = (slot_index[None, :] == jnp.arange(slot_total)[:, None]).astype(jnp.float32)
    strip_visit = jnp.repeat(ccd_visit[:, 0], per_ccd)
    placement = jnp.stack([strip_row, strip_col, strip_visit], axis=1).astype(jnp.float32)
    slot_meta = jnp.dot(chooser, placement, precision=largest_value).reshape(devices, capacity, 3)
    meta = jnp.zeros((devices, 8, columns), jnp.float32)
    meta = meta.at[:, 0:3, :capacity].set(jnp.swapaxes(slot_meta, 1, 2))
    meta = meta.at[:, 3, :VISITS].set(jnp.broadcast_to(local_count, (devices, VISITS)))
    meta = meta.at[:, 4, :VISITS].set(jnp.broadcast_to(local_load, (devices, VISITS)))
    body_rows = capacity * strip_rows
    weight_tiles = usable.reshape(strip_total, strip_rows * columns)
    weight_packed = jnp.dot(chooser, weight_tiles, precision=largest_value).reshape(
        devices, body_rows, columns
    )
    first = jnp.concatenate([weight_packed, meta], axis=1)
    got_first = lax.all_to_all(first, "patch", split_axis=0, concat_axis=0, tiled=True)
    convolved = convolve_all(exposures, kernel_coeffs)
    flux_tiles = (usable * convolved).reshape(strip_total, strip_rows * columns)
    flux_packed = jnp.dot(chooser, flux_tiles, precision=largest_value).reshape(
        devices, body_rows, columns
    )
    got_flux = lax.all_to_all(flux_packed, "patch", split_axis=0, concat_axis=0, tiled=True)
    got_meta = got_first[:, body_rows:, :]
    visit_count = jnp.sum(got_meta[:, 3, :VISITS], axis=0)
    visit_load = jnp.sum(got_meta[:, 4, :VISITS], axis=0)
    visit_weight = (visit_count + 1.0) / (visit_load + 1.0)
    slot_rows = got_meta[:, 0, :capacity].reshape(slot_total).astype(jnp.int32)
    slot_cols = got_meta[:, 1, :capacity].reshape(slot_total).astype(jnp.int32)
    slot_visit = got_meta[:, 2, :capacity].reshape(slot_total).astype(jnp.int32)
    slot_hot = (slot_visit[:, None] == jnp.arange(VISITS)[None, :]).astype(jnp.float32)
    slot_weight = jnp.sum(slot_hot * visit_weight[None, :], axis=1)
    weight_body = got_first[:, :body_rows, :].reshape(slot_total, strip_rows, columns)
    flux_body = got_flux.reshape(slot_total, strip_rows, columns)
    weight_body = weight_body * slot_weight[:, None, None]
    flux_body = flux_body * slot_weight[:, None, None]
    offsets = jnp.stack([slot_rows, slot_cols], axis=1)
    numerator, weight_map = place_slots(flux_body, weight_body, offsets, PH, PW)
    coadd_image = numerator / jnp.maximum(weight_map, 1.0)
    return (coadd_image[None], weight_map[None])


def solution(mesh):
    return jax.shard_map(
        shards,
        mesh=mesh,
        in_specs=(
            P(("band", "patch"), None, None),
            P(("band", "patch"), None, None),
            P(("band", "patch"), None, None),
            P(("band", "patch"), None, None),
            P(("band", "patch"), None),
            P(("band", "patch"), None),
            P(("band", "patch")),
            P(("band", "patch")),
        ),
        out_specs=(P(("band", "patch"), None, None), P(("band", "patch"), None, None)),
        check_vma=False,
    )
```

profile of v0, /device:TPU:0, one launch (start us, length us, event | category | flops | bytes accessed | tf_op | source)
XLA Modules:
  0.0 81.9 jit_solution(7379162448762953336)
XLA Ops:
  0.7 0.8 copy.70
  3.6 4.2 %multiply_reduce_fusion = f32[2,3,3,128,3,128]{5,3,4,2,1,0:T(8,128)} fusion(f32[2,3,3,3,3,128]{5,4,3,2,1,0:T(4,128)S(1)} %pad_maximum_fusion.2, f32[3,3,128,128]{3,2,1,0:T(8,128)} %constant.143.clone), kind=kLoop, calls=%fused_computation.20 | loop fusion | flops 4423680 | bytes 4211712 | tf_op jit(solution)/shard_map/reduce_sum | solution.py:74
  7.8 3.3 %copy.83 = f32[2,3,3,128,3,128]{3,5,4,2,1,0:T(8,128)S(1)} copy(f32[2,3,3,128,3,128]{5,3,4,2,1,0:T(8,128)} %multiply_reduce_fusion) | data formatting | bytes 7077888 | tf_op jit(solution)/shard_map/reduce_sum | solution.py:74
  11.1 1.0 %pad_bitcast_fusion = f32[2,35,8,128]{3,2,1,0:T(8,128)S(1)} fusion(f32[2,256,128]{2,1,0:T(8,128)} %param.18), kind=kLoop, calls=%fused_computation.37 | loop fusion | bytes 548864 | tf_op jit(solution)/shard_map/reshape | solution.py:58
  12.1 1.8 %fusion.22 = f32[2,32,128,9,8]{2,4,3,1,0:T(8,128)S(1)} fusion(f32[9,8,32,1,1]{2,1,0,4,3:T(8,128)} %constant.153, f32[2,32,8,128]{3,2,1,0:T(8,128)S(1)} %get-tuple-element.177, f32[2,32,8,128]{3,2,1,0:T(8,128)S(1)} %get-tuple-element.178, f32[2,32,8,128]{3,2,1,0:T(8,128)S(1)} %get-tuple-element.179, f32[2,32,8,128]{3,2,1,0:T(8,128)S(1)} %get-tuple-element.176), kind=kOutput, calls=%fused_computation.25 | convolution fusion | flops 114032640 | bytes 3417088 | tf_op jit(solution)/shard_map/kit,nqtx->nqkix/dot_general | solution.py:61
  14.0 2.3 %fusion.19 = f32[2,256,384]{2,1,0:T(8,128)S(1)} fusion(f32[2,9,128,384,1]{2,3,1,4,0:T(8,128)S(1)} %bitcast.101, f32[2,32,128,9,8]{2,4,3,1,0:T(8,128)S(1)} %fusion.22), kind=kOutput, calls=%fused_computation.23 | convolution fusion | flops 1358954496 | bytes 6684672 | tf_op jit(solution)/shard_map/nqkiy,nkyz->nqiz/dot_general | solution.py:76
  16.5 1.1 %select_reduce_fusion = (f32[2]{0:T(128)S(1)}, f32[2]{0:T(128)S(1)}) fusion(pred[2,256,128]{2,1,0:T(32,128)(4,1)S(1)} %get-tuple-element.171, f32[2,256,128]{2,1,0:T(8,128)} %param.19), kind=kLoop, calls=%fused_computation.44 | loop fusion | flops 262140 | bytes 327696 | tf_op jit(solution)/shard_map/reduce_sum | solution.py:134
  18.0 0.8 fusion.33
  19.9 0.8 %pad_maximum_fusion.1 = f32[8,136,128]{2,1,0:T(8,128)} fusion(f32[8,8,128]{2,1,0:T(8,128)S(1)} %scatter.14, f32[8,128,128]{2,1,0:T(8,128)S(1)} %reshape.332), kind=kLoop, calls=%fused_computation.33 | loop fusion | flops 139264 | bytes 1114112 | tf_op jit(solution)/shard_map/concatenate | solution.py:155
  20.8 7.3 %all-to-all-start.1 = ((f32[8,136,128]{2,1,0:T(8,128)}), f32[8,136,128]{2,1,0:T(8,128)S(1)}, u32[]{:S(2)}, u32[]{:S(2)}) async-start(f32[8,136,128]{2,1,0:T(8,128)} %pad_maximum_fusion.1), calls=%async_computation.1 | async-start | bytes 1114112 | tf_op jit(solution)/shard_map/all_to_all | solution.py:156
  28.5 0.9 %reshape.329 = f32[8,128,128]{2,1,0:T(8,128)} reshape(f32[128,1024]{1,0:T(8,128)S(1)} %fusion.35) | data formatting | bytes 1048576 | tf_op jit(solution)/shard_map/reshape | solution.py:159
  29.4 13.9 %all-to-all-done.1 = f32[8,136,128]{2,1,0:T(8,128)S(1)} async-done(((f32[8,136,128]{2,1,0:T(8,128)}), f32[8,136,128]{2,1,0:T(8,128)S(1)}, u32[]{:S(2)}, u32[]{:S(2)}) %all-to-all-start.1) | async-done | bytes 557088 | tf_op jit(solution)/shard_map/all_to_all | solution.py:156
  43.3 3.6 %all-to-all-start = ((f32[8,128,128]{2,1,0:T(8,128)}), f32[8,128,128]{2,1,0:T(8,128)S(1)}, u32[]{:S(2)}, u32[]{:S(2)}) async-start(f32[8,128,128]{2,1,0:T(8,128)} %reshape.329), calls=%async_computation | async-start | bytes 1048576 | tf_op jit(solution)/shard_map/all_to_all | solution.py:162
  47.3 14.3 %all-to-all-done = f32[8,128,128]{2,1,0:T(8,128)S(1)} async-done(((f32[8,128,128]{2,1,0:T(8,128)}), f32[8,128,128]{2,1,0:T(8,128)S(1)}, u32[]{:S(2)}, u32[]{:S(2)}) %all-to-all-start) | async-done | bytes 524320 | tf_op jit(solution)/shard_map/all_to_all | solution.py:162
  61.9 19.0 %while.16 = (s32[]{:T(128)}, f32[2,128,512]{1,2,0:T(8,128)S(1)}, f32[8,16,2,8,128]{4,3,2,1,0:T(8,128)S(1)}, s32[8,16,2]{1,0,2:T(8,128)S(1)}, s32[]{:T(128)}, /*index=5*/s32[]{:T(128)}) while((s32[]{:T(128)}, f32[2,128,512]{1,2,0:T(8,128)S(1)}, f32[8,16,2,8,128]{4,3,2,1,0:T(8,128)S(1)}, s32[8,16,2]{1,0,2:T(8,128)S(1)}, ...), condition=%wide.region_10.11_spmd.clone.clone, body=%wide.region_9.10_spmd.clone.clone.sunk | while | flops 403982464 | bytes 2246359 | solution.py:118
  62.0 1.5 %fusion.67 = f32[16,2,8,512]{3,2,1,0:T(8,128)S(1)} fusion(s32[16,128]{1,0:T(8,128)S(1)} %iota_add_fusion.4, f32[8,16,2,8,128]{4,3,2,1,0:T(8,128)S(1)} %get-tuple-element.237, s32[]{:T(128)} %get-tuple-element.229), kind=kOutput, calls=%fused_computation.5.clone.1 | convolution fusion | flops 202375168 | bytes 663556 | tf_op jit(solution)/shard_map/while/body/eval_jaxpr/vmwn,vny->vmwy/dot_general | solution.py:108
  64.3 1.5 %fusion.67 = f32[16,2,8,512]{3,2,1,0:T(8,128)S(1)} fusion(s32[16,128]{1,0:T(8,128)S(1)} %iota_add_fusion.4, f32[8,16,2,8,128]{4,3,2,1,0:T(8,128)S(1)} %get-tuple-element.237, s32[]{:T(128)} %get-tuple-element.229), kind=kOutput, calls=%fused_computation.5.clone.1 | convolution fusion | flops 202375168 | bytes 663556 | tf_op jit(solution)/shard_map/while/body/eval_jaxpr/vmwn,vny->vmwy/dot_general | solution.py:108
  66.7 1.5 %fusion.67 = f32[16,2,8,512]{3,2,1,0:T(8,128)S(1)} fusion(s32[16,128]{1,0:T(8,128)S(1)} %iota_add_fusion.4, f32[8,16,2,8,128]{4,3,2,1,0:T(8,128)S(1)} %get-tuple-element.237, s32[]{:T(128)} %get-tuple-element.229), kind=kOutput, calls=%fused_computation.5.clone.1 | convolution fusion | flops 202375168 | bytes 663556 | tf_op jit(solution)/shard_map/while/body/eval_jaxpr/vmwn,vny->vmwy/dot_general | solution.py:108
  69.1 1.5 %fusion.67 = f32[16,2,8,512]{3,2,1,0:T(8,128)S(1)} fusion(s32[16,128]{1,0:T(8,128)S(1)} %iota_add_fusion.4, f32[8,16,2,8,128]{4,3,2,1,0:T(8,128)S(1)} %get-tuple-element.237, s32[]{:T(128)} %get-tuple-element.229), kind=kOutput, calls=%fused_computation.5.clone.1 | convolution fusion | flops 202375168 | bytes 663556 | tf_op jit(solution)/shard_map/while/body/eval_jaxpr/vmwn,vny->vmwy/dot_general | solution.py:108
  71.5 1.5 %fusion.67 = f32[16,2,8,512]{3,2,1,0:T(8,128)S(1)} fusion(s32[16,128]{1,0:T(8,128)S(1)} %iota_add_fusion.4, f32[8,16,2,8,128]{4,3,2,1,0:T(8,128)S(1)} %get-tuple-element.237, s32[]{:T(128)} %get-tuple-element.229), kind=kOutput, calls=%fused_computation.5.clone.1 | convolution fusion | flops 202375168 | bytes 663556 | tf_op jit(solution)/shard_map/while/body/eval_jaxpr/vmwn,vny->vmwy/dot_general | solution.py:108
  73.8 1.5 %fusion.67 = f32[16,2,8,512]{3,2,1,0:T(8,128)S(1)} fusion(s32[16,128]{1,0:T(8,128)S(1)} %iota_add_fusion.4, f32[8,16,2,8,128]{4,3,2,1,0:T(8,128)S(1)} %get-tuple-element.237, s32[]{:T(128)} %get-tuple-element.229), kind=kOutput, calls=%fused_computation.5.clone.1 | convolution fusion | flops 202375168 | bytes 663556 | tf_op jit(solution)/shard_map/while/body/eval_jaxpr/vmwn,vny->vmwy/dot_general | solution.py:108
  76.2 1.5 %fusion.67 = f32[16,2,8,512]{3,2,1,0:T(8,128)S(1)} fusion(s32[16,128]{1,0:T(8,128)S(1)} %iota_add_fusion.4, f32[8,16,2,8,128]{4,3,2,1,0:T(8,128)S(1)} %get-tuple-element.237, s32[]{:T(128)} %get-tuple-element.229), kind=kOutput, calls=%fused_computation.5.clone.1 | convolution fusion | flops 202375168 | bytes 663556 | tf_op jit(solution)/shard_map/while/body/eval_jaxpr/vmwn,vny->vmwy/dot_general | solution.py:108
  78.6 1.5 %fusion.67 = f32[16,2,8,512]{3,2,1,0:T(8,128)S(1)} fusion(s32[16,128]{1,0:T(8,128)S(1)} %iota_add_fusion.4, f32[8,16,2,8,128]{4,3,2,1,0:T(8,128)S(1)} %get-tuple-element.237, s32[]{:T(128)} %get-tuple-element.229), kind=kOutput, calls=%fused_computation.5.clone.1 | convolution fusion | flops 202375168 | bytes 663556 | tf_op jit(solution)/shard_map/while/body/eval_jaxpr/vmwn,vny->vmwy/dot_general | solution.py:108
  81.1 0.8 slice_divide_fusion
  (97 shorter events, 12.0 us)
Async XLA Ops:
  14.0 2.3 %copy-start = (s32[2,256,128]{2,1,0:T(8,128)S(1)}, s32[2,256,128]{2,1,0:T(8,128)}, u32[]{:S(2)}) copy-start(s32[2,256,128]{2,1,0:T(8,128)} %param.20) | copy-start | bytes 786436
  14.0 3.7 %copy-start.2 = (s32[64,1]{0,1:T(1,128)S(1)}, s32[64,1]{0,1:T(1,128)}, u32[]{:S(2)}) copy-start(s32[64,1]{0,1:T(1,128)} %param.23) | copy-start | bytes 772
  14.0 3.8 %copy-start.1 = (s32[2,1]{0,1:T(1,128)S(1)}, s32[2,1]{0,1:T(1,128)}, u32[]{:S(2)}) copy-start(s32[2,1]{0,1:T(1,128)} %param.22) | copy-start | bytes 28
  20.8 22.5 %all-to-all-start.1 = ((f32[8,136,128]{2,1,0:T(8,128)}), f32[8,136,128]{2,1,0:T(8,128)S(1)}, u32[]{:S(2)}, u32[]{:S(2)}) async-start(f32[8,136,128]{2,1,0:T(8,128)} %pad_maximum_fusion.1), calls=%async_computation.1 | async-start | bytes 1114112 | tf_op jit(solution)/shard_map/all_to_all | solution.py:156
  43.3 18.3 %all-to-all-start = ((f32[8,128,128]{2,1,0:T(8,128)}), f32[8,128,128]{2,1,0:T(8,128)S(1)}, u32[]{:S(2)}, u32[]{:S(2)}) async-start(f32[8,128,128]{2,1,0:T(8,128)} %reshape.329), calls=%async_computation | async-start | bytes 1048576 | tf_op jit(solution)/shard_map/all_to_all | solution.py:162
where the time goes:
time: 82.4 us; the launch traced here: 81.9 us
  waiting for transfers between devices  28.2 us (34%)
  matrix products  22.9 us (28%)
  starting transfers between devices  10.9 us (13%)
  other arithmetic  9.37 us (11%)
  local copies, waits for them, and re-layouts  9.19 us (11%)
  between operations  0.95 us (1%)
    all_to_all x1, waiting for transfers between devices, shards(): lax.all_to_all(flux_packed, 'patch', split_axis=0, concat_axis=0, tiled=T...  14.3 us
    all_to_all x1, waiting for transfers between devices, shards(): lax.all_to_all(first, 'patch', split_axis=0, concat_axis=0, tiled=True)  13.9 us
    dot_general x8, matrix products, place_group(): jnp.einsum('vmwn,vny->vmwy', pixel_block_tile, column_selection, precisio...  11.7 us
    all_to_all x1, starting transfers between devices, shards(): lax.all_to_all(first, 'patch', split_axis=0, concat_axis=0, tiled=True)  7.31 us
    dot_general x8, matrix products, place_group(): jnp.einsum('gri,gkip->krp', row_select, broadened_width, precision=larges...  5.76 us
    reduce_sum x1, other arithmetic, convolve_all(): jnp.sum(col_ops[None, :, None, :, :, None, :] * fx[:, :, :, :, None, :, :...  4.17 us
    all_to_all x1, starting transfers between devices, shards(): lax.all_to_all(flux_packed, 'patch', split_axis=0, concat_axis=0, tiled=T...  3.64 us
    reduce_sum x1, local copies, waits for them, and re-layouts, convolve_all(): jnp.sum(col_ops[None, :, None, :, :, None, :] * fx[:, :, :, :, None, :, :...  3.31 us
  transfers between devices with their start and end apart: 2, of which 2 were waited for; matrix products, arithmetic and copies ran while one was open for 2% of the time, Pallas kernels for 0%

commit v1 on v0

--- a/solution.py
+++ b/solution.py
@@ -12,6 +12,17 @@
 gauss_widths = (0.75, 1.5, 3.0)
 largest_value = lax.Precision.HIGHEST
 mxu_value = lax.Precision.HIGH
+
+
+def in_blocks(x, dim, devices):
+    before, after = (x.shape[:dim], x.shape[dim + 1 :])
+    return jnp.moveaxis(x.reshape(*before, devices, -1, *after), dim, 0)
+
+
+def laid_out(blocks, dim):
+    dims = list(blocks.shape[1:])
+    dims[dim] *= blocks.shape[0]
+    return jnp.moveaxis(blocks, 0, dim).reshape(dims)
 
 
 def tap_table(kernel_half_width):
@@ -153,7 +164,14 @@
         devices, body_rows, columns
     )
     first = jnp.concatenate([weight_packed, meta], axis=1)
-    got_first = lax.all_to_all(first, "patch", split_axis=0, concat_axis=0, tiled=True)
+    size, index = (lax.axis_size("patch"), lax.axis_index("patch"))
+    blocks_2 = in_blocks(first, 0, size)
+    outs = [blocks_2[index]]
+    for hop in range(1, size):
+        sent = blocks_2[(index + hop) % size]
+        outs.append(lax.ppermute(sent, "patch", [(i_2, (i_2 + hop) % size) for i_2 in range(size)]))
+    blocks_2 = jnp.stack(outs)[(index - jnp.arange(size)) % size]
+    got_first = laid_out(blocks_2, 0)
     convolved = convolve_all(exposures, kernel_coeffs)
     flux_tiles = (usable * convolved).reshape(strip_total, strip_rows * columns)
     flux_packed = jnp.dot(chooser, flux_tiles, precision=largest_value).reshape(

time: 82.4 us -> 74.3 us (0.902)
  waiting for transfers between devices: 28.2 us -> 9.59 us
  starting transfers between devices: 10.9 us -> 21 us
    ppermute x0 -> x7, starting transfers between devices: none -> 16 us  [shards(): lax.ppermute(sent, 'patch', [(i_2, (i_2 + hop) % size) for i_2 in range(s...]
    all_to_all x1 -> x0, waiting for transfers between devices: 13.9 us -> none  [shards(): lax.all_to_all(first, 'patch', split_axis=0, concat_axis=0, tiled=True)]
    all_to_all x1, waiting for transfers between devices: 14.3 us -> 4.96 us  [shards(): lax.all_to_all(flux_packed, 'patch', split_axis=0, concat_axis=0, tiled=T...]
    all_to_all x1 -> x0, starting transfers between devices: 7.31 us -> none  [shards(): lax.all_to_all(first, 'patch', split_axis=0, concat_axis=0, tiled=True)]
    ppermute x0 -> x7, waiting for transfers between devices: none -> 4.63 us  [shards(): lax.ppermute(sent, 'patch', [(i_2, (i_2 + hop) % size) for i_2 in range(s...]
    all_to_all x1, starting transfers between devices: 3.64 us -> 5.03 us  [shards(): lax.all_to_all(flux_packed, 'patch', split_axis=0, concat_axis=0, tiled=T...]
  transfers between devices with their start and end apart: 2 -> 8, of which waited for: 2 -> 3; matrix products, arithmetic and copies ran while one was open for 2% -> 3% of each run, Pallas kernels for 0% -> 0%
where the time goes in v1:
time: 74.3 us; the launch traced here: 73.6 us
  matrix products  22.9 us (31%)
  starting transfers between devices  21 us (28%)
  local copies, waits for them, and re-layouts  9.81 us (13%)
  waiting for transfers between devices  9.59 us (13%)
  other arithmetic  8.82 us (12%)
  between operations  1.06 us (1%)
    ppermute x7, starting transfers between devices, shards(): lax.ppermute(sent, 'patch', [(i_2, (i_2 + hop) % size) for i_2 in range(s...  16 us
    dot_general x8, matrix products, place_group(): jnp.einsum('vmwn,vny->vmwy', pixel_block_tile, column_selection, precisio...  11.7 us
    dot_general x8, matrix products, place_group(): jnp.einsum('gri,gkip->krp', row_select, broadened_width, precision=larges...  5.73 us
    all_to_all x1, starting transfers between devices, shards(): lax.all_to_all(flux_packed, 'patch', split_axis=0, concat_axis=0, tiled=T...  5.03 us
    all_to_all x1, waiting for transfers between devices, shards(): lax.all_to_all(flux_packed, 'patch', split_axis=0, concat_axis=0, tiled=T...  4.96 us
    ppermute x7, waiting for transfers between devices, shards(): lax.ppermute(sent, 'patch', [(i_2, (i_2 + hop) % size) for i_2 in range(s...  4.63 us
    reduce_sum x1, other arithmetic, convolve_all(): jnp.sum(col_ops[None, :, None, :, :, None, :] * fx[:, :, :, :, None, :, :...  4.17 us
    reduce_sum x1, local copies, waits for them, and re-layouts, convolve_all(): jnp.sum(col_ops[None, :, None, :, :, None, :] * fx[:, :, :, :, None, :, :...  3.31 us
  transfers between devices with their start and end apart: 8, of which 3 were waited for; matrix products, arithmetic and copies ran while one was open for 3% of the time, Pallas kernels for 0%

profile of v1, /device:TPU:0, one launch (start us, length us, event | category | flops | bytes accessed | tf_op | source)
XLA Modules:
  0.0 73.6 jit_solution(8494723108381939552)
XLA Ops:
  3.6 4.2 %multiply_reduce_fusion = f32[2,3,3,128,3,128]{5,3,4,2,1,0:T(8,128)} fusion(f32[2,3,3,3,3,128]{5,4,3,2,1,0:T(4,128)S(1)} %pad_maximum_fusion.1, f32[3,3,128,128]{3,2,1,0:T(8,128)} %constant.206.clone), kind=kLoop, calls=%fused_computation.21 | loop fusion | flops 4423680 | bytes 4211712 | tf_op jit(solution)/shard_map/reduce_sum | solution.py:85
  7.8 3.3 %copy.68 = f32[2,3,3,128,3,128]{3,5,4,2,1,0:T(8,128)S(1)} copy(f32[2,3,3,128,3,128]{5,3,4,2,1,0:T(8,128)} %multiply_reduce_fusion) | data formatting | bytes 7077888 | tf_op jit(solution)/shard_map/reduce_sum | solution.py:85
  11.1 1.0 %pad_bitcast_fusion = f32[2,35,8,128]{3,2,1,0:T(8,128)S(1)} fusion(f32[2,256,128]{2,1,0:T(8,128)} %param.18), kind=kLoop, calls=%fused_computation.53 | loop fusion | bytes 548864 | tf_op jit(solution)/shard_map/reshape | solution.py:69
  12.1 1.8 %fusion.21 = f32[2,32,128,9,8]{2,4,3,1,0:T(8,128)S(1)} fusion(f32[9,8,32,1,1]{2,1,0,4,3:T(8,128)} %constant.216, f32[2,32,8,128]{3,2,1,0:T(8,128)S(1)} %get-tuple-element.179, f32[2,32,8,128]{3,2,1,0:T(8,128)S(1)} %get-tuple-element.180, f32[2,32,8,128]{3,2,1,0:T(8,128)S(1)} %get-tuple-element.181, f32[2,32,8,128]{3,2,1,0:T(8,128)S(1)} %get-tuple-element.178), kind=kOutput, calls=%fused_computation.34 | convolution fusion | flops 114032640 | bytes 3417088 | tf_op jit(solution)/shard_map/kit,nqtx->nqkix/dot_general | solution.py:72
  14.0 2.3 %fusion.18 = f32[2,256,384]{2,1,0:T(8,128)S(1)} fusion(f32[2,9,128,384,1]{2,3,1,4,0:T(8,128)S(1)} %bitcast.127, f32[2,32,128,9,8]{2,4,3,1,0:T(8,128)S(1)} %fusion.21), kind=kOutput, calls=%fused_computation.32 | convolution fusion | flops 1358954496 | bytes 6684672 | tf_op jit(solution)/shard_map/nqkiy,nkyz->nqiz/dot_general | solution.py:87
  16.5 1.1 %select_reduce_fusion = (f32[2]{0:T(128)S(1)}, f32[2]{0:T(128)S(1)}) fusion(pred[2,256,128]{2,1,0:T(32,128)(4,1)S(1)} %get-tuple-element.167, f32[2,256,128]{2,1,0:T(8,128)} %param.19), kind=kLoop, calls=%fused_computation.60 | loop fusion | flops 262140 | bytes 327696 | tf_op jit(solution)/shard_map/reduce_sum | solution.py:145
  20.0 5.1 %collective-permute-start.5 = (f32[1,136,128]{2,1,0:T(8,128)S(1)}, f32[1,136,128]{2,1,0:T(8,128)S(1)}, u32[]{:S(2)}, u32[]{:S(2)}) collective-permute-start(f32[1,136,128]{2,1,0:T(8,128)S(1)} %fusion.41), channel_id=1, source_target_pairs={{0,24},{4,28},{8,0},{12,4},{16,8},{20,12},{24,16},{28,20},{1,25},{... | collective-permute-start | bytes 208904 | tf_op jit(solution)/shard_map/ppermute | solution.py:172
  25.1 1.6 %collective-permute-start = (f32[1,136,128]{2,1,0:T(8,128)S(1)}, f32[1,136,128]{2,1,0:T(8,128)S(1)}, u32[]{:S(2)}, u32[]{:S(2)}) collective-permute-start(f32[1,136,128]{2,1,0:T(8,128)S(1)} %get-tuple-element.173), channel_id=1, source_target_pairs={{0,4},{4,8},{8,12},{12,16},{16,20},{20,24},{24,28},{28,0},{1,5},{5... | collective-permute-start | bytes 208904 | tf_op jit(solution)/shard_map/ppermute | solution.py:172
  26.7 1.0 %collective-permute-start.2 = (f32[1,136,128]{2,1,0:T(8,128)S(1)}, f32[1,136,128]{2,1,0:T(8,128)S(1)}, u32[]{:S(2)}, u32[]{:S(2)}) collective-permute-start(f32[1,136,128]{2,1,0:T(8,128)S(1)} %get-tuple-element.175), channel_id=1, source_target_pairs={{0,12},{4,16},{8,20},{12,24},{16,28},{20,0},{24,4},{28,8},{1,13},{... | collective-permute-start | bytes 208904 | tf_op jit(solution)/shard_map/ppermute | solution.py:172
  27.7 2.9 %collective-permute-start.3 = (f32[1,136,128]{2,1,0:T(8,128)S(1)}, f32[1,136,128]{2,1,0:T(8,128)S(1)}, u32[]{:S(2)}, u32[]{:S(2)}) collective-permute-start(f32[1,136,128]{2,1,0:T(8,128)S(1)} %get-tuple-element.176), channel_id=1, source_target_pairs={{0,16},{4,20},{8,24},{12,28},{16,0},{20,4},{24,8},{28,12},{1,17},{... | collective-permute-start | bytes 208904 | tf_op jit(solution)/shard_map/ppermute | solution.py:172
  31.9 5.0 %all-to-all-start = ((f32[8,128,128]{2,1,0:T(8,128)}), f32[8,128,128]{2,1,0:T(8,128)S(1)}, u32[]{:S(2)}, u32[]{:S(2)}) async-start(f32[8,128,128]{2,1,0:T(8,128)} %reshape.397), calls=%async_computation | async-start | bytes 1048576 | tf_op jit(solution)/shard_map/all_to_all | solution.py:180
  37.0 3.9 %collective-permute-start.4 = (f32[1,136,128]{2,1,0:T(8,128)S(1)}, f32[1,136,128]{2,1,0:T(8,128)S(1)}, u32[]{:S(2)}, u32[]{:S(2)}) collective-permute-start(f32[1,136,128]{2,1,0:T(8,128)S(1)} %get-tuple-element.177), channel_id=1, source_target_pairs={{0,20},{4,24},{8,28},{12,0},{16,4},{20,8},{24,12},{28,16},{1,21},{... | collective-permute-start | bytes 208904 | tf_op jit(solution)/shard_map/ppermute | solution.py:172
  40.9 1.5 %collective-permute-start.6 = (f32[1,136,128]{2,1,0:T(8,128)S(1)}, f32[1,136,128]{2,1,0:T(8,128)S(1)}, u32[]{:S(2)}, u32[]{:S(2)}) collective-permute-start(f32[1,136,128]{2,1,0:T(8,128)S(1)} %get-tuple-element.172), channel_id=1, source_target_pairs={{0,28},{4,0},{8,4},{12,8},{16,12},{20,16},{24,20},{28,24},{1,29},{... | collective-permute-start | bytes 208904 | tf_op jit(solution)/shard_map/ppermute | solution.py:172
  42.5 4.2 %collective-permute-done.4 = f32[1,136,128]{2,1,0:T(8,128)S(1)} collective-permute-done((f32[1,136,128]{2,1,0:T(8,128)S(1)}, f32[1,136,128]{2,1,0:T(8,128)S(1)}, u32[]{:S(2)}, u32[]{:S(2)}) %collective-permute-start.4) | collective-permute-done | bytes 69664 | tf_op jit(solution)/shard_map/ppermute | solution.py:172
  48.1 5.0 %all-to-all-done = f32[8,128,128]{2,1,0:T(8,128)S(1)} async-done(((f32[8,128,128]{2,1,0:T(8,128)}), f32[8,128,128]{2,1,0:T(8,128)S(1)}, u32[]{:S(2)}, u32[]{:S(2)}) %all-to-all-start) | async-done | bytes 524320 | tf_op jit(solution)/shard_map/all_to_all | solution.py:180
  53.3 19.2 %while.16 = (s32[]{:T(128)}, f32[2,128,512]{1,2,0:T(8,128)S(1)}, f32[8,16,2,8,128]{4,3,2,1,0:T(8,128)S(1)}, s32[8,16,2]{1,0,2:T(8,128)S(1)}, s32[]{:T(128)}, /*index=5*/s32[]{:T(128)}) while((s32[]{:T(128)}, f32[2,128,512]{1,2,0:T(8,128)S(1)}, f32[8,16,2,8,128]{4,3,2,1,0:T(8,128)S(1)}, s32[8,16,2]{1,0,2:T(8,128)S(1)}, ...), condition=%wide.region_10.11_spmd.clone.clone, body=%wide.region_9.10_spmd.clone.clone.sunk | while | flops 403982464 | bytes 2279127 | solution.py:129
  53.4 1.5 %fusion.78 = f32[16,2,8,512]{3,2,1,0:T(8,128)S(1)} fusion(s32[16,128]{1,0:T(8,128)S(1)} %iota_add_fusion.4, f32[8,16,2,8,128]{4,3,2,1,0:T(8,128)S(1)} %get-tuple-element.239, s32[]{:T(128)} %get-tuple-element.231), kind=kOutput, calls=%fused_computation.6.clone.1 | convolution fusion | flops 202375168 | bytes 663556 | tf_op jit(solution)/shard_map/while/body/eval_jaxpr/vmwn,vny->vmwy/dot_general | solution.py:119
  55.8 1.5 %fusion.78 = f32[16,2,8,512]{3,2,1,0:T(8,128)S(1)} fusion(s32[16,128]{1,0:T(8,128)S(1)} %iota_add_fusion.4, f32[8,16,2,8,128]{4,3,2,1,0:T(8,128)S(1)} %get-tuple-element.239, s32[]{:T(128)} %get-tuple-element.231), kind=kOutput, calls=%fused_computation.6.clone.1 | convolution fusion | flops 202375168 | bytes 663556 | tf_op jit(solution)/shard_map/while/body/eval_jaxpr/vmwn,vny->vmwy/dot_general | solution.py:119
  58.2 1.5 %fusion.78 = f32[16,2,8,512]{3,2,1,0:T(8,128)S(1)} fusion(s32[16,128]{1,0:T(8,128)S(1)} %iota_add_fusion.4, f32[8,16,2,8,128]{4,3,2,1,0:T(8,128)S(1)} %get-tuple-element.239, s32[]{:T(128)} %get-tuple-element.231), kind=kOutput, calls=%fused_computation.6.clone.1 | convolution fusion | flops 202375168 | bytes 663556 | tf_op jit(solution)/shard_map/while/body/eval_jaxpr/vmwn,vny->vmwy/dot_general | solution.py:119
  60.6 1.5 %fusion.78 = f32[16,2,8,512]{3,2,1,0:T(8,128)S(1)} fusion(s32[16,128]{1,0:T(8,128)S(1)} %iota_add_fusion.4, f32[8,16,2,8,128]{4,3,2,1,0:T(8,128)S(1)} %get-tuple-element.239, s32[]{:T(128)} %get-tuple-element.231), kind=kOutput, calls=%fused_computation.6.clone.1 | convolution fusion | flops 202375168 | bytes 663556 | tf_op jit(solution)/shard_map/while/body/eval_jaxpr/vmwn,vny->vmwy/dot_general | solution.py:119
  63.0 1.5 %fusion.78 = f32[16,2,8,512]{3,2,1,0:T(8,128)S(1)} fusion(s32[16,128]{1,0:T(8,128)S(1)} %iota_add_fusion.4, f32[8,16,2,8,128]{4,3,2,1,0:T(8,128)S(1)} %get-tuple-element.239, s32[]{:T(128)} %get-tuple-element.231), kind=kOutput, calls=%fused_computation.6.clone.1 | convolution fusion | flops 202375168 | bytes 663556 | tf_op jit(solution)/shard_map/while/body/eval_jaxpr/vmwn,vny->vmwy/dot_general | solution.py:119
  65.5 1.5 %fusion.78 = f32[16,2,8,512]{3,2,1,0:T(8,128)S(1)} fusion(s32[16,128]{1,0:T(8,128)S(1)} %iota_add_fusion.4, f32[8,16,2,8,128]{4,3,2,1,0:T(8,128)S(1)} %get-tuple-element.239, s32[]{:T(128)} %get-tuple-element.231), kind=kOutput, calls=%fused_computation.6.clone.1 | convolution fusion | flops 202375168 | bytes 663556 | tf_op jit(solution)/shard_map/while/body/eval_jaxpr/vmwn,vny->vmwy/dot_general | solution.py:119
  67.9 1.5 %fusion.78 = f32[16,2,8,512]{3,2,1,0:T(8,128)S(1)} fusion(s32[16,128]{1,0:T(8,128)S(1)} %iota_add_fusion.4, f32[8,16,2,8,128]{4,3,2,1,0:T(8,128)S(1)} %get-tuple-element.239, s32[]{:T(128)} %get-tuple-element.231), kind=kOutput, calls=%fused_computation.6.clone.1 | convolution fusion | flops 202375168 | bytes 663556 | tf_op jit(solution)/shard_map/while/body/eval_jaxpr/vmwn,vny->vmwy/dot_general | solution.py:119
  70.3 1.5 %fusion.78 = f32[16,2,8,512]{3,2,1,0:T(8,128)S(1)} fusion(s32[16,128]{1,0:T(8,128)S(1)} %iota_add_fusion.4, f32[8,16,2,8,128]{4,3,2,1,0:T(8,128)S(1)} %get-tuple-element.239, s32[]{:T(128)} %get-tuple-element.231), kind=kOutput, calls=%fused_computation.6.clone.1 | convolution fusion | flops 202375168 | bytes 663556 | tf_op jit(solution)/shard_map/while/body/eval_jaxpr/vmwn,vny->vmwy/dot_general | solution.py:119
  (127 shorter events, 16.6 us)
Async XLA Ops:
  14.0 2.3 %copy-start = (s32[2,256,128]{2,1,0:T(8,128)S(1)}, s32[2,256,128]{2,1,0:T(8,128)}, u32[]{:S(2)}) copy-start(s32[2,256,128]{2,1,0:T(8,128)} %param.20) | copy-start | bytes 786436
  14.0 3.7 %copy-start.2 = (s32[64,1]{0,1:T(1,128)S(1)}, s32[64,1]{0,1:T(1,128)}, u32[]{:S(2)}) copy-start(s32[64,1]{0,1:T(1,128)} %param.23) | copy-start | bytes 772
  14.0 3.8 %copy-start.1 = (s32[2,1]{0,1:T(1,128)S(1)}, s32[2,1]{0,1:T(1,128)}, u32[]{:S(2)}) copy-start(s32[2,1]{0,1:T(1,128)} %param.22) | copy-start | bytes 28
  20.0 26.7 %collective-permute-start.5 = (f32[1,136,128]{2,1,0:T(8,128)S(1)}, f32[1,136,128]{2,1,0:T(8,128)S(1)}, u32[]{:S(2)}, u32[]{:S(2)}) collective-permute-start(f32[1,136,128]{2,1,0:T(8,128)S(1)} %fusion.41), channel_id=1, source_target_pairs={{0,24},{4,28},{8,0},{12,4},{16,8},{20,12},{24,16},{28,20},{1,25},{... | collective-permute-start | bytes 208904 | tf_op jit(solution)/shard_map/ppermute | solution.py:172
  25.1 11.9 %collective-permute-start = (f32[1,136,128]{2,1,0:T(8,128)S(1)}, f32[1,136,128]{2,1,0:T(8,128)S(1)}, u32[]{:S(2)}, u32[]{:S(2)}) collective-permute-start(f32[1,136,128]{2,1,0:T(8,128)S(1)} %get-tuple-element.173), channel_id=1, source_target_pairs={{0,4},{4,8},{8,12},{12,16},{16,20},{20,24},{24,28},{28,0},{1,5},{5... | collective-permute-start | bytes 208904 | tf_op jit(solution)/shard_map/ppermute | solution.py:172
  26.7 14.2 %collective-permute-start.1 = (f32[1,136,128]{2,1,0:T(8,128)S(1)}, f32[1,136,128]{2,1,0:T(8,128)S(1)}, u32[]{:S(2)}, u32[]{:S(2)}) collective-permute-start(f32[1,136,128]{2,1,0:T(8,128)S(1)} %get-tuple-element.174), channel_id=1, source_target_pairs={{0,8},{4,12},{8,16},{12,20},{16,24},{20,28},{24,0},{28,4},{1,9},{5... | collective-permute-start | bytes 208904 | tf_op jit(solution)/shard_map/ppermute | solution.py:172
  26.7 15.7 %collective-permute-start.2 = (f32[1,136,128]{2,1,0:T(8,128)S(1)}, f32[1,136,128]{2,1,0:T(8,128)S(1)}, u32[]{:S(2)}, u32[]{:S(2)}) collective-permute-start(f32[1,136,128]{2,1,0:T(8,128)S(1)} %get-tuple-element.175), channel_id=1, source_target_pairs={{0,12},{4,16},{8,20},{12,24},{16,28},{20,0},{24,4},{28,8},{1,13},{... | collective-permute-start | bytes 208904 | tf_op jit(solution)/shard_map/ppermute | solution.py:172
  27.7 14.8 %collective-permute-start.3 = (f32[1,136,128]{2,1,0:T(8,128)S(1)}, f32[1,136,128]{2,1,0:T(8,128)S(1)}, u32[]{:S(2)}, u32[]{:S(2)}) collective-permute-start(f32[1,136,128]{2,1,0:T(8,128)S(1)} %get-tuple-element.176), channel_id=1, source_target_pairs={{0,16},{4,20},{8,24},{12,28},{16,0},{20,4},{24,8},{28,12},{1,17},{... | collective-permute-start | bytes 208904 | tf_op jit(solution)/shard_map/ppermute | solution.py:172
  31.9 21.1 %all-to-all-start = ((f32[8,128,128]{2,1,0:T(8,128)}), f32[8,128,128]{2,1,0:T(8,128)S(1)}, u32[]{:S(2)}, u32[]{:S(2)}) async-start(f32[8,128,128]{2,1,0:T(8,128)} %reshape.397), calls=%async_computation | async-start | bytes 1048576 | tf_op jit(solution)/shard_map/all_to_all | solution.py:180
  37.0 9.7 %collective-permute-start.4 = (f32[1,136,128]{2,1,0:T(8,128)S(1)}, f32[1,136,128]{2,1,0:T(8,128)S(1)}, u32[]{:S(2)}, u32[]{:S(2)}) collective-permute-start(f32[1,136,128]{2,1,0:T(8,128)S(1)} %get-tuple-element.177), channel_id=1, source_target_pairs={{0,20},{4,24},{8,28},{12,0},{16,4},{20,8},{24,12},{28,16},{1,21},{... | collective-permute-start | bytes 208904 | tf_op jit(solution)/shard_map/ppermute | solution.py:172
  40.9 6.2 %collective-permute-start.6 = (f32[1,136,128]{2,1,0:T(8,128)S(1)}, f32[1,136,128]{2,1,0:T(8,128)S(1)}, u32[]{:S(2)}, u32[]{:S(2)}) collective-permute-start(f32[1,136,128]{2,1,0:T(8,128)S(1)} %get-tuple-element.172), channel_id=1, source_target_pairs={{0,28},{4,0},{8,4},{12,8},{16,12},{20,16},{24,20},{28,24},{1,29},{... | collective-permute-start | bytes 208904 | tf_op jit(solution)/shard_map/ppermute | solution.py:172
